TPU v7x, 256 devices: a whole 4x4x8 slice. The times are simulated.
256 devices in a mesh: rep: 16 (over x_lo, y, core), shard: 16 (over z, x_hi).
Axes of the slice: x: 4 (x_hi: 2, x_lo: 2; x = x_hi * 2 + x_lo), y: 4, z: 8, core: 2. Of those that a mesh axis runs over, the one named last changes fastest.
Arguments:
- activations: bfloat16 [32768, 4096], P(('rep', 'shard')), may hold values from -24 to 24
- cotangent: bfloat16 [32768, 896], P(('rep', 'shard')), may hold values from -0.099609375 to 0.099609375
- weight: bfloat16 [16, 4096, 896], P('rep', 'shard'), may hold values from -6 to 6
- momentum: bfloat16 [16, 4096, 896], P('rep', 'shard'), may hold values from -6 to 6
- step_index: int32 [1], replicated, may hold values from 0 to 999
Outputs:
- averaged: bfloat16 [16, 4096, 896], P('rep', 'shard')
- momentum_new: bfloat16 [16, 4096, 896], P('rep', 'shard')
All inputs are finite; a program needn't handle non-finite values.
Results may differ from a plain program's by a relative error of at most 0.012.
Values may be sent and summed in bfloat16 or wider, within the bound.
No kernel may reach another device: no remote copies, remote signals or barrier semaphores. Data moves between devices by JAX's collectives and lax.ppermute only.
A program may use at most 64 MiB of HBM per device.

v0:
```python
import jax
import jax.numpy as jnp
from jax import lax
from jax.sharding import PartitionSpec as P


def shortened(value):

    def short(part):
        return part.astype(jnp.bfloat16) if part.dtype == jnp.float32 else part

    return jax.tree.map(short, value)


def from_behind(value, axis, by):
    count = lax.axis_size(axis)
    return lax.ppermute(value, axis, [(i, (i + by) % count) for i in range(count)])


def shifter(distance):
    return lambda tensor_value: jax.tree.map(
        lambda part, own: part.astype(own.dtype),
        from_behind(shortened(tensor_value), "rep", distance),
        tensor_value,
    )


def per_device(activations, cotangent, weight, momentum, step_index):
    gradient = lax.psum_scatter(
        jnp.einsum("tr,tc->rc", activations, cotangent, preferred_element_type=jnp.float32).astype(
            jnp.bfloat16
        ),
        "shard",
        scatter_dimension=0,
        tiled=True,
    ).astype(jnp.float32)
    momentum_new = (0.9 * momentum[0].astype(jnp.float32) + gradient).astype(jnp.bfloat16)
    half_step = (weight[0].astype(jnp.float32) - 0.5 * momentum_new.astype(jnp.float32)).astype(
        jnp.bfloat16
    )
    levels = lax.axis_size("rep").bit_length() - 1
    branches = [shifter(1 << bit_number) for bit_number in range(levels)]
    received = lax.switch(step_index[0] % levels, branches, half_step)
    averaged = (0.5 * (half_step.astype(jnp.float32) + received.astype(jnp.float32))).astype(
        jnp.bfloat16
    )
    return (averaged[None], momentum_new[None])


def solution(mesh):
    return jax.shard_map(
        per_device,
        mesh=mesh,
        in_specs=(
            P(("rep", "shard"), None),
            P(("rep", "shard"), None),
            P("rep", "shard", None),
            P("rep", "shard", None),
            P(),
        ),
        out_specs=(P("rep", "shard", None), P("rep", "shard", None)),
        check_vma=False,
    )
```

profile of v0, /device:TPU:4, one launch (start us, length us, event | category | flops | bytes accessed | tf_op | source)
XLA Modules:
  0.0 261.2 jit_solution(17753010331895007366)
XLA Ops:
  7.2 0.0 copy-start
  7.2 0.0 copy-start.1
  7.2 0.0 copy-start.2
  7.2 0.0 reduce-scatter.2.cloned.1.call-start
  7.2 1.1 copy-done
  8.4 6.0 %convolution_convert_fusion = bf16[4096,896]{1,0:T(8,128)(2,1)} fusion(bf16[128,4096]{1,0:T(8,128)(2,1)S(1)} %copy-done, bf16[128,896]{1,0:T(8,128)(2,1)} %param.10), kind=kOutput, calls=%fused_computation | convolution fusion | flops 943194112 | bytes 8617984 | tf_op jit(solution)/shard_map/tr,tc->rc/dot_general | solution.py:30
  14.4 0.0 reduce-scatter.2.cloned.1.call-update
  15.1 224.2 %reduce-scatter.2.cloned.1.call-done = bf16[256,896]{1,0:T(8,128)(2,1)} async-done(((bf16[4096,896]{1,0:T(8,128)(2,1)}), bf16[256,896]{1,0:T(8,128)(2,1)}) %reduce-scatter.2.cloned.1.call-update) | async-done | bytes 458768 | tf_op jit(solution)/shard_map/reduce_scatter | solution.py:29
  239.2 0.0 copy-done.1
  239.2 0.0 copy-done.2
  239.2 2.0 fusion.3
  241.3 11.2 %conditional.4 = (bf16[256,896]{1,0:T(8,128)(2,1)}) conditional(s32[]{:T(128)} %clamp.3, bf16[256,896]{1,0:T(8,128)(2,1)S(1)} %get-tuple-element.18, bf16[256,896]{1,0:T(8,128)(2,1)S(1)} %get-tuple-element.18, bf16[256,896]{1,0:T(8,128)(2,1)S(1)} %get-tuple-element.18, bf16[256,896]{1,0:T(8,128)(2,1)S(1)} %get-tuple-element.18), branch_computations={%region_1.2_spmd, %region_2.3_spmd, %region_3.4_spmd, %region_4.5_... | conditional | bytes 1835056
  241.3 1.5 collective-permute-start.1
  242.8 9.7 %collective-permute-done.1 = bf16[256,896]{1,0:T(8,128)(2,1)} collective-permute-done((bf16[256,896]{1,0:T(8,128)(2,1)S(1)}, bf16[256,896]{1,0:T(8,128)(2,1)}, u32[]{:S(2)}, u32[]{:S(2)}) %collective-permute-start.1) | collective-permute-done | bytes 458784 | tf_op jit(solution)/shard_map/cond/branch_1_fun/ppermute | solution.py:17
  252.5 1.9 fusion.2
Async XLA Ops:
  7.2 1.2 copy-start
  7.2 232.1 %copy-start.1 = (bf16[1,256,896]{2,1,0:T(8,128)(2,1)S(1)}, bf16[1,256,896]{2,1,0:T(8,128)(2,1)}, u32[]{:S(2)}) copy-start(bf16[1,256,896]{2,1,0:T(8,128)(2,1)} %param.12) | copy-start | bytes 1376260
  7.2 232.1 %copy-start.2 = (bf16[1,256,896]{2,1,0:T(8,128)(2,1)S(1)}, bf16[1,256,896]{2,1,0:T(8,128)(2,1)}, u32[]{:S(2)}) copy-start(bf16[1,256,896]{2,1,0:T(8,128)(2,1)} %param.11) | copy-start | bytes 1376260
  7.2 232.0 %reduce-scatter.2.cloned.1.call-start = ((), (), s32[]{:S(2)}) async-start(), calls=%async_computation.1 | async-start | bytes 7798784 | tf_op jit(solution)/shard_map/reduce_scatter | solution.py:29
  241.3 11.2 %collective-permute-start.1 = (bf16[256,896]{1,0:T(8,128)(2,1)S(1)}, bf16[256,896]{1,0:T(8,128)(2,1)}, u32[]{:S(2)}, u32[]{:S(2)}) collective-permute-start(bf16[256,896]{1,0:T(8,128)(2,1)S(1)} %param.1), channel_id=1, source_target_pairs={{0,32},{16,48},{32,64},{48,80},{64,96},{80,112},{96,128},{112,144}... | collective-permute-start | bytes 1376264 | tf_op jit(solution)/shard_map/cond/branch_1_fun/ppermute | solution.py:17
Sparse Core Ops, SparseCore 0:
  14.5 224.6 reduce-scatter.1
where the time goes:
time: 263 us; the launch traced here: 261 us
  waiting for transfers between devices  234 us (89%)
  between operations  14.7 us (6%)
  matrix products  5.99 us (2%)
  other arithmetic  3.95 us (2%)
    reduce_scatter x1, waiting for transfers between devices, per_device(): lax.psum_scatter(jnp.einsum('tr,tc->rc', activations, cotangent, preferre...  224 us
    ppermute x1, waiting for transfers between devices, from_behind(): lax.ppermute(value, axis, [(i, (i + by) % count) for i in range(count)])  9.7 us
    dot_general x1, matrix products, per_device(): jnp.einsum('tr,tc->rc', activations, cotangent, preferred_element_type=jn...  5.99 us
  transfers between devices with their start and end apart: 2, of which 2 were waited for; matrix products, arithmetic and copies ran while one was open for 0% of the time, Pallas kernels for 0%

commit v1 on v0

--- a/solution.py
+++ b/solution.py
@@ -1,7 +1,10 @@
+import numpy as np
 import jax
 import jax.numpy as jnp
 from jax import lax
-from jax.sharding import PartitionSpec as P
+from jax.sharding import Mesh, PartitionSpec as P
+
+PAIR = 2
 
 
 def shortened(value):
@@ -25,15 +28,27 @@
     )
 
 
+def pair_gradient(activations, cotangent, rows):
+    tokens, width = activations.shape
+    nz = lax.axis_size("z")
+    pair_rows = rows * PAIR
+    columns = activations.reshape(tokens, nz, pair_rows).transpose(1, 0, 2)
+    columns = lax.all_to_all(columns, "z", 0, 0)
+    cot_blocks = lax.all_gather(cotangent, "z")
+    partial = jnp.einsum(
+        "ktr,ktc->krc", columns, cot_blocks, preferred_element_type=jnp.float32
+    ).astype(jnp.bfloat16)
+    return jnp.sum(partial.astype(jnp.float32), axis=0)
+
+
 def per_device(activations, cotangent, weight, momentum, step_index):
-    gradient = lax.psum_scatter(
-        jnp.einsum("tr,tc->rc", activations, cotangent, preferred_element_type=jnp.float32).astype(
-            jnp.bfloat16
-        ),
-        "shard",
-        scatter_dimension=0,
-        tiled=True,
-    ).astype(jnp.float32)
+    rows = weight.shape[1]
+    pair_sum = pair_gradient(activations, cotangent, rows)
+    side = lax.axis_index("xh")
+    own = lax.dynamic_slice_in_dim(pair_sum, side * rows, rows, 0)
+    other = lax.dynamic_slice_in_dim(pair_sum, (1 - side) * rows, rows, 0)
+    swapped = lax.ppermute(other.astype(jnp.bfloat16), "xh", [(0, 1), (1, 0)])
+    gradient = own + swapped.astype(jnp.float32)
     momentum_new = (0.9 * momentum[0].astype(jnp.float32) + gradient).astype(jnp.bfloat16)
     half_step = (weight[0].astype(jnp.float32) - 0.5 * momentum_new.astype(jnp.float32)).astype(
         jnp.bfloat16
@@ -48,16 +63,21 @@
 
 
 def solution(mesh):
+    n_rep, n_shard = mesh.devices.shape
+    split = Mesh(
+        np.asarray(mesh.devices).reshape(n_rep, n_shard // PAIR, PAIR), ("rep", "z", "xh")
+    )
+    tokens = ("rep", "z", "xh")
     return jax.shard_map(
         per_device,
-        mesh=mesh,
+        mesh=split,
         in_specs=(
-            P(("rep", "shard"), None),
-            P(("rep", "shard"), None),
-            P("rep", "shard", None),
-            P("rep", "shard", None),
+            P(tokens, None),
+            P(tokens, None),
+            P("rep", ("z", "xh"), None),
+            P("rep", ("z", "xh"), None),
             P(),
         ),
-        out_specs=(P("rep", "shard", None), P("rep", "shard", None)),
+        out_specs=(P("rep", ("z", "xh"), None), P("rep", ("z", "xh"), None)),
         check_vma=False,
     )

time: 263 us -> 106 us (0.40)
  waiting for transfers between devices: 234 us -> 68.9 us
  starting transfers between devices: 1.53 us -> 12.2 us
    reduce_scatter x1 -> x0, waiting for transfers between devices: 224 us -> none  [per_device(): lax.psum_scatter(jnp.einsum('tr,tc->rc', activations, cotangent, preferre...]
    all_to_all x0 -> x1, waiting for transfers between devices: none -> 38.6 us  [pair_gradient(): columns = lax.all_to_all(columns, 'z', 0, 0)]
    ppermute x0 -> x1, waiting for transfers between devices: none -> 11 us  [per_device(): swapped = lax.ppermute(other.astype(jnp.bfloat16), 'xh', [(0, 1), (1, 0)])]
    all_gather x0 -> x1, waiting for transfers between devices: none -> 9.44 us  [pair_gradient(): cot_blocks = lax.all_gather(cotangent, 'z')]
    all_to_all x0 -> x1, starting transfers between devices: none -> 8.47 us  [pair_gradient(): columns = lax.all_to_all(columns, 'z', 0, 0)]
  transfers between devices with their start and end apart: 2 -> 4, of which waited for: 2 -> 4; matrix products, arithmetic and copies ran while one was open for 0% -> 2% of each run, Pallas kernels for 0% -> 0%
where the time goes in v1:
time: 106 us
  waiting for transfers between devices  68.9 us (65%)
  between operations  14.7 us (14%)
  starting transfers between devices  12.2 us (12%)
  other arithmetic  3.98 us (4%)
  matrix products  3.69 us (3%)
  local copies, waits for them, and re-layouts  2.34 us (2%)
    all_to_all x1, waiting for transfers between devices, pair_gradient(): columns = lax.all_to_all(columns, 'z', 0, 0)  38.6 us
    ppermute x1, waiting for transfers between devices, per_device(): swapped = lax.ppermute(other.astype(jnp.bfloat16), 'xh', [(0, 1), (1, 0)])  11 us
    all_gather x1, waiting for transfers between devices, pair_gradient(): cot_blocks = lax.all_gather(cotangent, 'z')  9.44 us
    ppermute x1, waiting for transfers between devices, from_behind(): lax.ppermute(value, axis, [(i, (i + by) % count) for i in range(count)])  9.15 us
    all_to_all x1, starting transfers between devices, pair_gradient(): columns = lax.all_to_all(columns, 'z', 0, 0)  8.47 us
    dot_general x1, matrix products, pair_gradient(): jnp.einsum('ktr,ktc->krc', columns, cot_blocks, preferred_element_type=jn...  3.69 us
    ppermute x1, starting transfers between devices, from_behind(): lax.ppermute(value, axis, [(i, (i + by) % count) for i in range(count)])  3.12 us
    unnamed x3, local copies, waits for them, and re-layouts  2.28 us
  transfers between devices with their start and end apart: 4, of which 4 were waited for; matrix products, arithmetic and copies ran while one was open for 2% of the time, Pallas kernels for 0%

profile of v1, /device:TPU:4, one launch (start us, length us, event | category | flops | bytes accessed | tf_op | source)
XLA Modules:
  0.0 105.8 jit_solution(16160748529235046342)
XLA Ops:
  7.2 0.0 all-gather.3.cloned.1.call-start
  7.2 0.7 all-gather.3.cloned.1.call-update
  7.9 2.3 %copy.7 = bf16[128,4096]{0,1:T(8,128)(2,1)} copy(bf16[128,4096]{1,0:T(8,128)(2,1)} %param.9) | data formatting | bytes 2097152 | tf_op args[0]
  10.2 8.5 %all-to-all-start = ((bf16[8,128,512]{1,2,0:T(8,128)(2,1)}), bf16[8,128,512]{1,2,0:T(8,128)(2,1)S(1)}, u32[]{:S(2)}, u32[]{:S(2)}) async-start(bf16[8,128,512]{1,2,0:T(8,128)(2,1)} %bitcast.3), calls=%async_computation | async-start | bytes 2097152 | tf_op jit(solution)/shard_map/all_to_all | solution.py:36
  18.6 38.6 %all-to-all-done = bf16[8,128,512]{1,2,0:T(8,128)(2,1)S(1)} async-done(((bf16[8,128,512]{1,2,0:T(8,128)(2,1)}), bf16[8,128,512]{1,2,0:T(8,128)(2,1)S(1)}, u32[]{:S(2)}, u32[]{:S(2)}) %all-to-all-start) | async-done | bytes 1048608 | tf_op jit(solution)/shard_map/all_to_all | solution.py:36
  57.2 9.4 %all-gather.3.cloned.1.call-done = bf16[1024,896]{1,0:T(8,128)(2,1)} async-done(((bf16[128,896]{1,0:T(8,128)(2,1)}), bf16[1024,896]{1,0:T(8,128)(2,1)}) %all-gather.3.cloned.1.call-update) | async-done | bytes 1835024 | tf_op jit(solution)/shard_map/all_gather | solution.py:37
  66.7 0.0 copy-start
  66.7 3.7 %convert_reduce_fusion = f32[512,896]{1,0:T(8,128)S(1)} fusion(bf16[8,128,512]{1,2,0:T(8,128)(2,1)S(1)} %all-to-all-done, bf16[8,128,896]{2,1,0:T(8,128)(2,1)} %bitcast.22), kind=kOutput, calls=%fused_computation | convolution fusion | flops 950075392 | bytes 4718592 | tf_op jit(solution)/shard_map/ktr,ktc->krc/dot_general | solution.py:38
  70.4 0.1 dynamic-slice_convert_fusion
  70.4 0.6 collective-permute-start.4
  71.7 11.0 %collective-permute-done.4 = bf16[256,896]{1,0:T(8,128)(2,1)S(1)} collective-permute-done((bf16[256,896]{1,0:T(8,128)(2,1)S(1)}, bf16[256,896]{1,0:T(8,128)(2,1)S(1)}, u32[]{:S(2)}, u32[]{:S(2)}) %collective-permute-start.4) | collective-permute-done | bytes 458784 | tf_op jit(solution)/shard_map/ppermute | solution.py:50
  82.7 0.0 copy-done
  82.7 2.1 %fusion = (bf16[256,896]{1,0:T(8,128)(2,1)S(1)}, bf16[256,896]{1,0:T(8,128)(2,1)}) fusion(bf16[1,256,896]{2,1,0:T(8,128)(2,1)S(1)} %copy-done, bf16[256,896]{1,0:T(8,128)(2,1)S(1)} %collective-permute-done.4, f32[512,896]{1,0:T(8,128)S(1)} %convert_reduce_fusion, s32[]{:T(128)S(6)} %select_n.13, bf16[1,256,896]{2,1,0:T(8,128)(2,1)} %param.12), kind=kLoop, calls=%fused_computation.2 | loop fusion | flops 2523136 | bytes 3211268 | tf_op jit(solution)/shard_map/convert_element_type | solution.py:53
  84.8 12.3 %conditional.4 = (bf16[256,896]{1,0:T(8,128)(2,1)}) conditional(s32[]{:T(128)} %clamp.3, bf16[256,896]{1,0:T(8,128)(2,1)S(1)} %get-tuple-element.17, bf16[256,896]{1,0:T(8,128)(2,1)S(1)} %get-tuple-element.17, bf16[256,896]{1,0:T(8,128)(2,1)S(1)} %get-tuple-element.17, bf16[256,896]{1,0:T(8,128)(2,1)S(1)} %get-tuple-element.17), branch_computations={%region_1.2_spmd, %region_2.3_spmd, %region_3.4_spmd, %region_4.5_... | conditional | bytes 1835056
  84.8 3.1 %collective-permute-start.2 = (bf16[256,896]{1,0:T(8,128)(2,1)S(1)}, bf16[256,896]{1,0:T(8,128)(2,1)}, u32[]{:S(2)}, u32[]{:S(2)}) collective-permute-start(bf16[256,896]{1,0:T(8,128)(2,1)S(1)} %param.2), channel_id=1, source_target_pairs={{0,64},{16,80},{32,96},{48,112},{64,128},{80,144},{96,160},{112,17... | collective-permute-start | bytes 1376264 | tf_op jit(solution)/shard_map/cond/branch_2_fun/ppermute | solution.py:20
  87.9 9.2 %collective-permute-done.2 = bf16[256,896]{1,0:T(8,128)(2,1)} collective-permute-done((bf16[256,896]{1,0:T(8,128)(2,1)S(1)}, bf16[256,896]{1,0:T(8,128)(2,1)}, u32[]{:S(2)}, u32[]{:S(2)}) %collective-permute-start.2) | collective-permute-done | bytes 458784 | tf_op jit(solution)/shard_map/cond/branch_2_fun/ppermute | solution.py:20
  97.1 1.9 %fusion.2 = bf16[1,256,896]{2,1,0:T(8,128)(2,1)} fusion(bf16[256,896]{1,0:T(8,128)(2,1)} %get-tuple-element.19, bf16[256,896]{1,0:T(8,128)(2,1)S(1)} %get-tuple-element.17), kind=kLoop, calls=%fused_computation.7 | loop fusion | flops 1146880 | bytes 1376256 | tf_op jit(solution)/shard_map/broadcast_in_dim | solution.py:62
Async XLA Ops:
  7.2 59.5 %all-gather.3.cloned.1.call-start = ((), (), s32[]{:S(2)}) async-start(), calls=%async_computation.1 | async-start | bytes 2064384 | tf_op jit(solution)/shard_map/all_gather | solution.py:37
  10.2 47.1 %all-to-all-start = ((bf16[8,128,512]{1,2,0:T(8,128)(2,1)}), bf16[8,128,512]{1,2,0:T(8,128)(2,1)S(1)}, u32[]{:S(2)}, u32[]{:S(2)}) async-start(bf16[8,128,512]{1,2,0:T(8,128)(2,1)} %bitcast.3), calls=%async_computation | async-start | bytes 2097152 | tf_op jit(solution)/shard_map/all_to_all | solution.py:36
  66.7 16.0 %copy-start = (bf16[1,256,896]{2,1,0:T(8,128)(2,1)S(1)}, bf16[1,256,896]{2,1,0:T(8,128)(2,1)}, u32[]{:S(2)}) copy-start(bf16[1,256,896]{2,1,0:T(8,128)(2,1)} %param.11) | copy-start | bytes 1376260
  70.4 12.3 %collective-permute-start.4 = (bf16[256,896]{1,0:T(8,128)(2,1)S(1)}, bf16[256,896]{1,0:T(8,128)(2,1)S(1)}, u32[]{:S(2)}, u32[]{:S(2)}) collective-permute-start(bf16[256,896]{1,0:T(8,128)(2,1)S(1)} %dynamic-slice_convert_fusion), channel_id=1, source_target_pairs={{0,1},{1,0},{2,3},{3,2},{4,5},{5,4},{6,7},{7,6},{8,9},{9,8},{10,11... | collective-permute-start | bytes 1376264 | tf_op jit(solution)/shard_map/ppermute | solution.py:50
  84.8 12.3 %collective-permute-start.2 = (bf16[256,896]{1,0:T(8,128)(2,1)S(1)}, bf16[256,896]{1,0:T(8,128)(2,1)}, u32[]{:S(2)}, u32[]{:S(2)}) collective-permute-start(bf16[256,896]{1,0:T(8,128)(2,1)S(1)} %param.2), channel_id=1, source_target_pairs={{0,64},{16,80},{32,96},{48,112},{64,128},{80,144},{96,160},{112,17... | collective-permute-start | bytes 1376264 | tf_op jit(solution)/shard_map/cond/branch_2_fun/ppermute | solution.py:20
Sparse Core Ops, SparseCore 0:
  9.8 56.8 all-gather.2

commit v2 on v1

--- a/solution.py
+++ b/solution.py
@@ -7,25 +7,9 @@
 PAIR = 2
 
 
-def shortened(value):
-
-    def short(part):
-        return part.astype(jnp.bfloat16) if part.dtype == jnp.float32 else part
-
-    return jax.tree.map(short, value)
-
-
 def from_behind(value, axis, by):
     count = lax.axis_size(axis)
     return lax.ppermute(value, axis, [(i, (i + by) % count) for i in range(count)])
-
-
-def shifter(distance):
-    return lambda tensor_value: jax.tree.map(
-        lambda part, own: part.astype(own.dtype),
-        from_behind(shortened(tensor_value), "rep", distance),
-        tensor_value,
-    )
 
 
 def pair_gradient(activations, cotangent, rows):
@@ -41,21 +25,52 @@
     return jnp.sum(partial.astype(jnp.float32), axis=0)
 
 
+def from_behind_across(value, distance):
+    n_rep, n_side = lax.axis_size("rep"), lax.axis_size("xh")
+    pairs = [
+        (r * n_side + j, ((r + distance) % n_rep) * n_side + (n_side - 1 - j))
+        for r in range(n_rep)
+        for j in range(n_side)
+    ]
+    return lax.ppermute(value, ("rep", "xh"), pairs)
+
+
+def tail_sends(distance):
+    def run(own, other):
+        swapped = lax.ppermute(other, "xh", [(0, 1), (1, 0)])
+        return swapped, from_behind(own, "rep", distance), from_behind_across(other, distance)
+
+    return run
+
+
 def per_device(activations, cotangent, weight, momentum, step_index):
     rows = weight.shape[1]
+    levels = lax.axis_size("rep").bit_length() - 1
+    choice = step_index[0] % levels
+    distances = [1 << bit_number for bit_number in range(levels)]
+    held = jnp.stack([weight[0], momentum[0]])
+    partner = lax.switch(
+        choice, [lambda v, by=by: from_behind(v, "rep", by) for by in distances], held
+    )
     pair_sum = pair_gradient(activations, cotangent, rows)
     side = lax.axis_index("xh")
     own = lax.dynamic_slice_in_dim(pair_sum, side * rows, rows, 0)
-    other = lax.dynamic_slice_in_dim(pair_sum, (1 - side) * rows, rows, 0)
-    swapped = lax.ppermute(other.astype(jnp.bfloat16), "xh", [(0, 1), (1, 0)])
-    gradient = own + swapped.astype(jnp.float32)
-    momentum_new = (0.9 * momentum[0].astype(jnp.float32) + gradient).astype(jnp.bfloat16)
-    half_step = (weight[0].astype(jnp.float32) - 0.5 * momentum_new.astype(jnp.float32)).astype(
-        jnp.bfloat16
+    other = lax.dynamic_slice_in_dim(pair_sum, (1 - side) * rows, rows, 0).astype(jnp.bfloat16)
+    swapped, partner_own, partner_other = lax.switch(
+        choice, [tail_sends(by) for by in distances], own.astype(jnp.bfloat16), other
     )
-    levels = lax.axis_size("rep").bit_length() - 1
-    branches = [shifter(1 << bit_number) for bit_number in range(levels)]
-    received = lax.switch(step_index[0] % levels, branches, half_step)
+
+    def step(w, m, gradient):
+        moment = (0.9 * m.astype(jnp.float32) + gradient).astype(jnp.bfloat16)
+        half = (w.astype(jnp.float32) - 0.5 * moment.astype(jnp.float32)).astype(jnp.bfloat16)
+        return moment, half
+
+    momentum_new, half_step = step(weight[0], momentum[0], own + swapped.astype(jnp.float32))
+    unused, received = step(
+        partner[0],
+        partner[1],
+        partner_own.astype(jnp.float32) + partner_other.astype(jnp.float32),
+    )
     averaged = (0.5 * (half_step.astype(jnp.float32) + received.astype(jnp.float32))).astype(
         jnp.bfloat16
     )

time: 106 us -> 110 us (1.038); the launches traced: 106 us -> 107 us
  starting transfers between devices: 12.2 us -> 13.4 us
    all_to_all x1, waiting for transfers between devices: 38.6 us -> 22.7 us  [pair_gradient(): columns = lax.all_to_all(columns, 'z', 0, 0)]
    ppermute x1 -> x2, waiting for transfers between devices: 9.15 us -> 25 us  [from_behind(): lax.ppermute(value, axis, [(i, (i + by) % count) for i in range(count)])]
    ppermute x1 -> x2, starting transfers between devices: 0.61 us -> 4.78 us  [the longest x1 2.99 us: run(): swapped = lax.ppermute(other, 'xh', [(0, 1), (1, 0)])]
    ppermute x1 -> x2, starting transfers between devices: 3.12 us -> 0.17 us  [from_behind(): lax.ppermute(value, axis, [(i, (i + by) % count) for i in range(count)])]
    convert_element_type x1 -> x0, other arithmetic: 2.06 us -> none  [per_device(): (weight[0].astype(jnp.float32) - 0.5 * momentum_new.astype(jnp.float32))....]
    add x0 -> x1, other arithmetic: none -> 1.11 us  [per_device(): partner_own.astype(jnp.float32) + partner_other.astype(jnp.float32)]
    ppermute x1 -> x2, waiting for transfers between devices: 11 us -> 11.1 us  [the longest x1 11.1 us: from_behind_across(): return lax.ppermute(value, ('rep', 'xh'), pairs)]
    unnamed x3 -> x5, local copies, waits for them, and re-layouts: 2.28 us -> 2.36 us
  transfers between devices with their start and end apart: 4 -> 6, of which waited for: 4 -> 5; matrix products, arithmetic and copies ran while one was open for 2% -> 3% of each run, Pallas kernels for 0% -> 0%
where the time goes in v2:
time: 110 us; the launch traced here: 107 us
  waiting for transfers between devices  68.9 us (63%)
  between operations  14.8 us (13%)
  starting transfers between devices  13.4 us (12%)
  other arithmetic  4.08 us (4%)
  matrix products  3.66 us (3%)
  local copies, waits for them, and re-layouts  2.46 us (2%)
    ppermute x2, waiting for transfers between devices, from_behind(): lax.ppermute(value, axis, [(i, (i + by) % count) for i in range(count)])  25 us
    all_to_all x1, waiting for transfers between devices, pair_gradient(): columns = lax.all_to_all(columns, 'z', 0, 0)  22.7 us
    ppermute x1, waiting for transfers between devices, from_behind_across(): return lax.ppermute(value, ('rep', 'xh'), pairs)  11.1 us
    all_gather x1, waiting for transfers between devices, pair_gradient(): cot_blocks = lax.all_gather(cotangent, 'z')  9.44 us
    all_to_all x1, starting transfers between devices, pair_gradient(): columns = lax.all_to_all(columns, 'z', 0, 0)  8.47 us
    dot_general x1, matrix products, pair_gradient(): jnp.einsum('ktr,ktc->krc', columns, cot_blocks, preferred_element_type=jn...  3.66 us
    ppermute x1, starting transfers between devices, run(): swapped = lax.ppermute(other, 'xh', [(0, 1), (1, 0)])  2.99 us
    broadcast_in_dim x1, other arithmetic, per_device(): return (averaged[None], momentum_new[None])  2.87 us
  transfers between devices with their start and end apart: 6, of which 5 were waited for; matrix products, arithmetic and copies ran while one was open for 3% of the time, Pallas kernels for 0%

profile of v2, /device:TPU:4, one launch (start us, length us, event | category | flops | bytes accessed | tf_op | source)
XLA Modules:
  0.0 107.4 jit_solution(3106481550512152583)
XLA Ops:
  7.2 0.0 all-gather.3.cloned.1.call-start
  7.2 0.7 all-gather.3.cloned.1.call-update
  7.9 0.0 copy-start
  7.9 0.0 copy-start.1
  7.9 2.3 %copy.7 = bf16[128,4096]{0,1:T(8,128)(2,1)} copy(bf16[128,4096]{1,0:T(8,128)(2,1)} %param.13) | data formatting | bytes 2097152 | tf_op args[0]
  10.3 8.5 %all-to-all-start = ((bf16[8,128,512]{1,2,0:T(8,128)(2,1)}), bf16[8,128,512]{1,2,0:T(8,128)(2,1)S(1)}, u32[]{:S(2)}, u32[]{:S(2)}) async-start(bf16[8,128,512]{1,2,0:T(8,128)(2,1)} %bitcast.3), calls=%async_computation | async-start | bytes 2097152 | tf_op jit(solution)/shard_map/all_to_all | solution.py:20
  19.4 0.0 copy-done
  19.4 0.0 copy-done.1
  19.4 0.1 pad_maximum_fusion
  19.5 15.1 %conditional.5 = (bf16[2,256,896]{2,1,0:T(8,128)(2,1)}) conditional(s32[]{:T(128)} %clamp.4, bf16[2,256,896]{2,1,0:T(8,128)(2,1)S(1)} %pad_maximum_fusion, bf16[2,256,896]{2,1,0:T(8,128)(2,1)S(1)} %pad_maximum_fusion, bf16[2,256,896]{2,1,0:T(8,128)(2,1)S(1)} %pad_maximum_fusion, ...), branch_computations={%region_5.6_spmd, %region_6.7_spmd, %region_7.8_spmd, %region_8.9_... | conditional | bytes 3670064 | solution.py:52
  19.5 0.1 collective-permute-start
  19.6 15.0 %collective-permute-done = bf16[2,256,896]{2,1,0:T(8,128)(2,1)} collective-permute-done((bf16[2,256,896]{2,1,0:T(8,128)(2,1)S(1)}, bf16[2,256,896]{2,1,0:T(8,128)(2,1)}, u32[]{:S(2)}, u32[]{:S(2)}) %collective-permute-start) | collective-permute-done | bytes 917536 | tf_op jit(solution)/shard_map/cond/branch_0_fun/ppermute | solution.py:12
  34.7 22.7 %all-to-all-done = bf16[8,128,512]{1,2,0:T(8,128)(2,1)S(1)} async-done(((bf16[8,128,512]{1,2,0:T(8,128)(2,1)}), bf16[8,128,512]{1,2,0:T(8,128)(2,1)S(1)}, u32[]{:S(2)}, u32[]{:S(2)}) %all-to-all-start) | async-done | bytes 1048608 | tf_op jit(solution)/shard_map/all_to_all | solution.py:20
  57.4 9.4 %all-gather.3.cloned.1.call-done = bf16[1024,896]{1,0:T(8,128)(2,1)} async-done(((bf16[128,896]{1,0:T(8,128)(2,1)}), bf16[1024,896]{1,0:T(8,128)(2,1)}) %all-gather.3.cloned.1.call-update) | async-done | bytes 1835024 | tf_op jit(solution)/shard_map/all_gather | solution.py:21
  66.8 3.7 %convert_reduce_fusion = f32[512,896]{1,0:T(8,128)S(1)} fusion(bf16[8,128,512]{1,2,0:T(8,128)(2,1)S(1)} %all-to-all-done, bf16[8,128,896]{2,1,0:T(8,128)(2,1)} %bitcast.33), kind=kOutput, calls=%fused_computation.4 | convolution fusion | flops 950075392 | bytes 4718592 | tf_op jit(solution)/shard_map/ktr,ktc->krc/dot_general | solution.py:22
  70.5 0.1 dynamic-slice_convert_fusion
  70.6 27.1 %conditional.6 = (bf16[256,896]{1,0:T(8,128)(2,1)}, f32[256,896]{1,0:T(8,128)S(1)}, bf16[256,896]{1,0:T(8,128)(2,1)}) conditional(s32[]{:T(128)} %clamp.4, (bf16[256,896]{1,0:T(8,128)(2,1)S(1)}, bf16[256,896]{1,0:T(8,128)(2,1)S(1)}) %tuple.62, (bf16[256,896]{1,0:T(8,128)(2,1)S(1)}, ...), branch_computations={%region_1.2_spmd, %region_2.3_spmd, %region_3.4_spmd, %region_4.5_... | conditional | flops 688128 | bytes 7340176
  70.6 0.1 collective-permute-start.4
  70.7 1.8 %collective-permute-start.5 = (bf16[256,896]{1,0:T(8,128)(2,1)S(1)}, bf16[256,896]{1,0:T(8,128)(2,1)S(1)}, u32[]{:S(2)}, u32[]{:S(2)}) collective-permute-start(bf16[256,896]{1,0:T(8,128)(2,1)S(1)} %get-tuple-element.39), channel_id=1, source_target_pairs={{0,17},{1,16},{16,33},{17,32},{32,49},{33,48},{48,65},{49,64},{64,... | collective-permute-start | bytes 1376264 | tf_op jit(solution)/shard_map/cond/branch_0_fun/ppermute | solution.py:35
  72.5 3.0 %collective-permute-start.6 = (bf16[256,896]{1,0:T(8,128)(2,1)S(1)}, bf16[256,896]{1,0:T(8,128)(2,1)}, u32[]{:S(2)}, u32[]{:S(2)}) collective-permute-start(bf16[256,896]{1,0:T(8,128)(2,1)S(1)} %get-tuple-element.39), channel_id=1, source_target_pairs={{0,1},{1,0},{2,3},{3,2},{4,5},{5,4},{6,7},{7,6},{8,9},{9,8},{10,11... | collective-permute-start | bytes 1376264 | tf_op jit(solution)/shard_map/cond/branch_0_fun/ppermute | solution.py:40
  75.5 9.9 %collective-permute-done.4 = bf16[256,896]{1,0:T(8,128)(2,1)} collective-permute-done((bf16[256,896]{1,0:T(8,128)(2,1)S(1)}, bf16[256,896]{1,0:T(8,128)(2,1)}, u32[]{:S(2)}, u32[]{:S(2)}) %collective-permute-start.4) | collective-permute-done | bytes 458784 | tf_op jit(solution)/shard_map/cond/branch_0_fun/ppermute | solution.py:12
  85.4 11.1 %collective-permute-done.5 = bf16[256,896]{1,0:T(8,128)(2,1)S(1)} collective-permute-done((bf16[256,896]{1,0:T(8,128)(2,1)S(1)}, bf16[256,896]{1,0:T(8,128)(2,1)S(1)}, u32[]{:S(2)}, u32[]{:S(2)}) %collective-permute-start.5) | collective-permute-done | bytes 458784 | tf_op jit(solution)/shard_map/cond/branch_0_fun/ppermute | solution.py:35
  96.6 1.1 %convert_add_fusion = f32[256,896]{1,0:T(8,128)S(1)} fusion(bf16[256,896]{1,0:T(8,128)(2,1)S(1)} %collective-permute-done.5, bf16[256,896]{1,0:T(8,128)(2,1)} %collective-permute-done.4), kind=kLoop, calls=%fused_computation | loop fusion | flops 688128 | bytes 1835008 | tf_op jit(solution)/shard_map/add | solution.py:72
  97.7 0.0 collective-permute-done.6
  97.7 2.9 %fusion.5 = (bf16[1,256,896]{2,1,0:T(8,128)(2,1)}, bf16[256,896]{1,0:T(8,128)(2,1)}) fusion(f32[256,896]{1,0:T(8,128)S(1)} %get-tuple-element.51, bf16[2,256,896]{2,1,0:T(8,128)(2,1)} %get-tuple-element.73, bf16[1,256,896]{2,1,0:T(8,128)(2,1)} %param.15, bf16[256,896]{1,0:T(8,128)(2,1)} %get-tuple-element.56, f32[512,896]{1,0:T(8,128)S(1)} %convert_reduce_fusion, ...), kind=kLoop, calls=%fused_computation.18 | loop fusion | flops 5734400 | bytes 5046276 | tf_op jit(solution)/shard_map/broadcast_in_dim | solution.py:77
Async XLA Ops:
  7.2 59.6 %all-gather.3.cloned.1.call-start = ((), (), s32[]{:S(2)}) async-start(), calls=%async_computation.1 | async-start | bytes 2064384 | tf_op jit(solution)/shard_map/all_gather | solution.py:21
  7.9 11.5 %copy-start = (bf16[1,256,896]{2,1,0:T(8,128)(2,1)S(1)}, bf16[1,256,896]{2,1,0:T(8,128)(2,1)}, u32[]{:S(2)}) copy-start(bf16[1,256,896]{2,1,0:T(8,128)(2,1)} %param.16) | copy-start | bytes 1376260
  7.9 11.5 %copy-start.1 = (bf16[1,256,896]{2,1,0:T(8,128)(2,1)S(1)}, bf16[1,256,896]{2,1,0:T(8,128)(2,1)}, u32[]{:S(2)}) copy-start(bf16[1,256,896]{2,1,0:T(8,128)(2,1)} %param.15) | copy-start | bytes 1376260
  10.3 47.1 %all-to-all-start = ((bf16[8,128,512]{1,2,0:T(8,128)(2,1)}), bf16[8,128,512]{1,2,0:T(8,128)(2,1)S(1)}, u32[]{:S(2)}, u32[]{:S(2)}) async-start(bf16[8,128,512]{1,2,0:T(8,128)(2,1)} %bitcast.3), calls=%async_computation | async-start | bytes 2097152 | tf_op jit(solution)/shard_map/all_to_all | solution.py:20
  19.5 15.1 %collective-permute-start = (bf16[2,256,896]{2,1,0:T(8,128)(2,1)S(1)}, bf16[2,256,896]{2,1,0:T(8,128)(2,1)}, u32[]{:S(2)}, u32[]{:S(2)}) collective-permute-start(bf16[2,256,896]{2,1,0:T(8,128)(2,1)S(1)} %param.4), channel_id=1, source_target_pairs={{0,16},{16,32},{32,48},{48,64},{64,80},{80,96},{96,112},{112,128},... | collective-permute-start | bytes 2752520 | tf_op jit(solution)/shard_map/cond/branch_0_fun/ppermute | solution.py:12
  70.6 14.8 %collective-permute-start.4 = (bf16[256,896]{1,0:T(8,128)(2,1)S(1)}, bf16[256,896]{1,0:T(8,128)(2,1)}, u32[]{:S(2)}, u32[]{:S(2)}) collective-permute-start(bf16[256,896]{1,0:T(8,128)(2,1)S(1)} %get-tuple-element.38), channel_id=1, source_target_pairs={{0,16},{16,32},{32,48},{48,64},{64,80},{80,96},{96,112},{112,128},... | collective-permute-start | bytes 1376264 | tf_op jit(solution)/shard_map/cond/branch_0_fun/ppermute | solution.py:12
  70.7 25.9 %collective-permute-start.5 = (bf16[256,896]{1,0:T(8,128)(2,1)S(1)}, bf16[256,896]{1,0:T(8,128)(2,1)S(1)}, u32[]{:S(2)}, u32[]{:S(2)}) collective-permute-start(bf16[256,896]{1,0:T(8,128)(2,1)S(1)} %get-tuple-element.39), channel_id=1, source_target_pairs={{0,17},{1,16},{16,33},{17,32},{32,49},{33,48},{48,65},{49,64},{64,... | collective-permute-start | bytes 1376264 | tf_op jit(solution)/shard_map/cond/branch_0_fun/ppermute | solution.py:35
  72.5 25.2 %collective-permute-start.6 = (bf16[256,896]{1,0:T(8,128)(2,1)S(1)}, bf16[256,896]{1,0:T(8,128)(2,1)}, u32[]{:S(2)}, u32[]{:S(2)}) collective-permute-start(bf16[256,896]{1,0:T(8,128)(2,1)S(1)} %get-tuple-element.39), channel_id=1, source_target_pairs={{0,1},{1,0},{2,3},{3,2},{4,5},{5,4},{6,7},{7,6},{8,9},{9,8},{10,11... | collective-permute-start | bytes 1376264 | tf_op jit(solution)/shard_map/cond/branch_0_fun/ppermute | solution.py:40
Sparse Core Ops, SparseCore 0:
  9.8 56.9 all-gather.2

commit v3 on v1

--- a/solution.py
+++ b/solution.py
@@ -35,10 +35,9 @@
     columns = activations.reshape(tokens, nz, pair_rows).transpose(1, 0, 2)
     columns = lax.all_to_all(columns, "z", 0, 0)
     cot_blocks = lax.all_gather(cotangent, "z")
-    partial = jnp.einsum(
-        "ktr,ktc->krc", columns, cot_blocks, preferred_element_type=jnp.float32
-    ).astype(jnp.bfloat16)
-    return jnp.sum(partial.astype(jnp.float32), axis=0)
+    return jnp.einsum(
+        "ktr,ktc->rc", columns, cot_blocks, preferred_element_type=jnp.float32
+    )
 
 
 def per_device(activations, cotangent, weight, momentum, step_index):

time: 106 us -> 106 us (level)
  no operation moved by 1% of the time
where the time goes in v3:
time: 106 us; the launch traced here: 105 us
  waiting for transfers between devices  68.9 us (65%)
  between operations  14.7 us (14%)
  starting transfers between devices  12.2 us (12%)
  other arithmetic  3.98 us (4%)
  matrix products  2.8 us (3%)
  local copies, waits for them, and re-layouts  2.34 us (2%)
    all_to_all x1, waiting for transfers between devices, pair_gradient(): columns = lax.all_to_all(columns, 'z', 0, 0)  38.6 us
    ppermute x1, waiting for transfers between devices, per_device(): swapped = lax.ppermute(other.astype(jnp.bfloat16), 'xh', [(0, 1), (1, 0)])  11 us
    all_gather x1, waiting for transfers between devices, pair_gradient(): cot_blocks = lax.all_gather(cotangent, 'z')  9.44 us
    ppermute x1, waiting for transfers between devices, from_behind(): lax.ppermute(value, axis, [(i, (i + by) % count) for i in range(count)])  9.14 us
    all_to_all x1, starting transfers between devices, pair_gradient(): columns = lax.all_to_all(columns, 'z', 0, 0)  8.47 us
    ppermute x1, starting transfers between devices, from_behind(): lax.ppermute(value, axis, [(i, (i + by) % count) for i in range(count)])  3.13 us
    dot_general x1, matrix products, pair_gradient(): jnp.einsum('ktr,ktc->rc', columns, cot_blocks, preferred_element_type=jnp...  2.8 us
    unnamed x3, local copies, waits for them, and re-layouts  2.28 us
  transfers between devices with their start and end apart: 4, of which 4 were waited for; matrix products, arithmetic and copies ran while one was open for 2% of the time, Pallas kernels for 0%

profile of v3, /device:TPU:4, one launch (start us, length us, event | category | flops | bytes accessed | tf_op | source)
XLA Modules:
  0.0 104.9 jit_solution(1668594664860690032)
XLA Ops:
  7.2 0.0 all-gather.3.cloned.1.call-start
  7.2 0.7 all-gather.3.cloned.1.call-update
  7.9 2.3 %copy.7 = bf16[128,4096]{0,1:T(8,128)(2,1)} copy(bf16[128,4096]{1,0:T(8,128)(2,1)} %param.9) | data formatting | bytes 2097152 | tf_op args[0]
  10.2 8.5 %all-to-all-start = ((bf16[8,128,512]{1,2,0:T(8,128)(2,1)}), bf16[8,128,512]{1,2,0:T(8,128)(2,1)S(1)}, u32[]{:S(2)}, u32[]{:S(2)}) async-start(bf16[8,128,512]{1,2,0:T(8,128)(2,1)} %bitcast.3), calls=%async_computation | async-start | bytes 2097152 | tf_op jit(solution)/shard_map/all_to_all | solution.py:36
  18.6 38.6 %all-to-all-done = bf16[8,128,512]{1,2,0:T(8,128)(2,1)S(1)} async-done(((bf16[8,128,512]{1,2,0:T(8,128)(2,1)}), bf16[8,128,512]{1,2,0:T(8,128)(2,1)S(1)}, u32[]{:S(2)}, u32[]{:S(2)}) %all-to-all-start) | async-done | bytes 1048608 | tf_op jit(solution)/shard_map/all_to_all | solution.py:36
  57.2 9.4 %all-gather.3.cloned.1.call-done = bf16[1024,896]{1,0:T(8,128)(2,1)} async-done(((bf16[128,896]{1,0:T(8,128)(2,1)}), bf16[1024,896]{1,0:T(8,128)(2,1)}) %all-gather.3.cloned.1.call-update) | async-done | bytes 1835024 | tf_op jit(solution)/shard_map/all_gather | solution.py:37
  66.7 0.0 copy-start
  66.7 2.8 %convolution_bitcast_fusion = f32[512,896]{1,0:T(8,128)S(1)} fusion(bf16[8,128,512]{1,2,0:T(8,128)(2,1)S(1)} %all-to-all-done, bf16[8,128,896]{2,1,0:T(8,128)(2,1)} %bitcast.24), kind=kOutput, calls=%fused_computation | convolution fusion | flops 939524096 | bytes 4718592 | tf_op jit(solution)/shard_map/ktr,ktc->rc/dot_general | solution.py:38
  69.5 0.1 dynamic-slice_convert_fusion
  69.6 0.6 collective-permute-start.4
  70.8 11.0 %collective-permute-done.4 = bf16[256,896]{1,0:T(8,128)(2,1)S(1)} collective-permute-done((bf16[256,896]{1,0:T(8,128)(2,1)S(1)}, bf16[256,896]{1,0:T(8,128)(2,1)S(1)}, u32[]{:S(2)}, u32[]{:S(2)}) %collective-permute-start.4) | collective-permute-done | bytes 458784 | tf_op jit(solution)/shard_map/ppermute | solution.py:49
  81.8 0.0 copy-done
  81.8 2.1 %fusion = (bf16[256,896]{1,0:T(8,128)(2,1)S(1)}, bf16[256,896]{1,0:T(8,128)(2,1)}) fusion(bf16[1,256,896]{2,1,0:T(8,128)(2,1)S(1)} %copy-done, bf16[256,896]{1,0:T(8,128)(2,1)S(1)} %collective-permute-done.4, f32[512,896]{1,0:T(8,128)S(1)} %convolution_bitcast_fusion, s32[]{:T(128)S(6)} %select_n.13, bf16[1,256,896]{2,1,0:T(8,128)(2,1)} %param.12), kind=kLoop, calls=%fused_computation.2 | loop fusion | flops 2523136 | bytes 3211268 | tf_op jit(solution)/shard_map/convert_element_type | solution.py:52
  83.9 12.3 %conditional.4 = (bf16[256,896]{1,0:T(8,128)(2,1)}) conditional(s32[]{:T(128)} %clamp.3, bf16[256,896]{1,0:T(8,128)(2,1)S(1)} %get-tuple-element.17, bf16[256,896]{1,0:T(8,128)(2,1)S(1)} %get-tuple-element.17, bf16[256,896]{1,0:T(8,128)(2,1)S(1)} %get-tuple-element.17, bf16[256,896]{1,0:T(8,128)(2,1)S(1)} %get-tuple-element.17), branch_computations={%region_0.1_spmd, %region_1.2_spmd, %region_2.3_spmd, %region_3.4_... | conditional | bytes 1835056
  83.9 3.1 %collective-permute-start.2 = (bf16[256,896]{1,0:T(8,128)(2,1)S(1)}, bf16[256,896]{1,0:T(8,128)(2,1)}, u32[]{:S(2)}, u32[]{:S(2)}) collective-permute-start(bf16[256,896]{1,0:T(8,128)(2,1)S(1)} %param.2), channel_id=1, source_target_pairs={{0,64},{16,80},{32,96},{48,112},{64,128},{80,144},{96,160},{112,17... | collective-permute-start | bytes 1376264 | tf_op jit(solution)/shard_map/cond/branch_2_fun/ppermute | solution.py:20
  87.0 9.1 %collective-permute-done.2 = bf16[256,896]{1,0:T(8,128)(2,1)} collective-permute-done((bf16[256,896]{1,0:T(8,128)(2,1)S(1)}, bf16[256,896]{1,0:T(8,128)(2,1)}, u32[]{:S(2)}, u32[]{:S(2)}) %collective-permute-start.2) | collective-permute-done | bytes 458784 | tf_op jit(solution)/shard_map/cond/branch_2_fun/ppermute | solution.py:20
  96.2 1.9 %fusion.2 = bf16[1,256,896]{2,1,0:T(8,128)(2,1)} fusion(bf16[256,896]{1,0:T(8,128)(2,1)} %get-tuple-element.19, bf16[256,896]{1,0:T(8,128)(2,1)S(1)} %get-tuple-element.17), kind=kLoop, calls=%fused_computation.7 | loop fusion | flops 1146880 | bytes 1376256 | tf_op jit(solution)/shard_map/broadcast_in_dim | solution.py:61
Async XLA Ops:
  7.2 59.5 %all-gather.3.cloned.1.call-start = ((), (), s32[]{:S(2)}) async-start(), calls=%async_computation.1 | async-start | bytes 2064384 | tf_op jit(solution)/shard_map/all_gather | solution.py:37
  10.2 47.1 %all-to-all-start = ((bf16[8,128,512]{1,2,0:T(8,128)(2,1)}), bf16[8,128,512]{1,2,0:T(8,128)(2,1)S(1)}, u32[]{:S(2)}, u32[]{:S(2)}) async-start(bf16[8,128,512]{1,2,0:T(8,128)(2,1)} %bitcast.3), calls=%async_computation | async-start | bytes 2097152 | tf_op jit(solution)/shard_map/all_to_all | solution.py:36
  66.7 15.1 %copy-start = (bf16[1,256,896]{2,1,0:T(8,128)(2,1)S(1)}, bf16[1,256,896]{2,1,0:T(8,128)(2,1)}, u32[]{:S(2)}) copy-start(bf16[1,256,896]{2,1,0:T(8,128)(2,1)} %param.11) | copy-start | bytes 1376260
  69.6 12.3 %collective-permute-start.4 = (bf16[256,896]{1,0:T(8,128)(2,1)S(1)}, bf16[256,896]{1,0:T(8,128)(2,1)S(1)}, u32[]{:S(2)}, u32[]{:S(2)}) collective-permute-start(bf16[256,896]{1,0:T(8,128)(2,1)S(1)} %dynamic-slice_convert_fusion), channel_id=1, source_target_pairs={{0,1},{1,0},{2,3},{3,2},{4,5},{5,4},{6,7},{7,6},{8,9},{9,8},{10,11... | collective-permute-start | bytes 1376264 | tf_op jit(solution)/shard_map/ppermute | solution.py:49
  83.9 12.3 %collective-permute-start.2 = (bf16[256,896]{1,0:T(8,128)(2,1)S(1)}, bf16[256,896]{1,0:T(8,128)(2,1)}, u32[]{:S(2)}, u32[]{:S(2)}) collective-permute-start(bf16[256,896]{1,0:T(8,128)(2,1)S(1)} %param.2), channel_id=1, source_target_pairs={{0,64},{16,80},{32,96},{48,112},{64,128},{80,144},{96,160},{112,17... | collective-permute-start | bytes 1376264 | tf_op jit(solution)/shard_map/cond/branch_2_fun/ppermute | solution.py:20
Sparse Core Ops, SparseCore 0:
  9.8 56.8 all-gather.2

commit v4 on v3

v4 whole, which is shorter than its diff:
```python
import numpy as np
import jax
import jax.numpy as jnp
from jax import lax
from jax.sharding import Mesh, PartitionSpec as P

PAIR = 2
HALVES = 2


def from_behind(value, axis, by):
    count = lax.axis_size(axis)
    return lax.ppermute(value, axis, [(i, (i + by) % count) for i in range(count)])


def pair_gradient(activations, cotangent, rows):
    tokens, width = activations.shape
    nz = lax.axis_size("z")
    pair_rows = rows * PAIR
    columns = activations.reshape(tokens, nz, pair_rows).transpose(1, 0, 2)
    columns = lax.all_to_all(columns, "z", 0, 0)
    cot_blocks = lax.all_gather(cotangent, "z")
    return jnp.einsum(
        "ktr,ktc->rc", columns, cot_blocks, preferred_element_type=jnp.float32
    )


def tail(distance, halves):
    def run(own, other, weight, momentum):
        rows = own.shape[0]
        step = rows // halves
        averaged, momentum_new = [], []
        for lo in range(0, rows, step):
            swapped = lax.ppermute(other[lo : lo + step], "xh", [(0, 1), (1, 0)])
            gradient = own[lo : lo + step] + swapped.astype(jnp.float32)
            moment = (0.9 * momentum[lo : lo + step].astype(jnp.float32) + gradient).astype(
                jnp.bfloat16
            )
            half_step = (
                weight[lo : lo + step].astype(jnp.float32) - 0.5 * moment.astype(jnp.float32)
            ).astype(jnp.bfloat16)
            received = from_behind(half_step, "rep", distance)
            averaged.append(
                (0.5 * (half_step.astype(jnp.float32) + received.astype(jnp.float32))).astype(
                    jnp.bfloat16
                )
            )
            momentum_new.append(moment)
        return jnp.concatenate(averaged), jnp.concatenate(momentum_new)

    return run


def per_device(activations, cotangent, weight, momentum, step_index):
    rows = weight.shape[1]
    pair_sum = pair_gradient(activations, cotangent, rows)
    side = lax.axis_index("xh")
    own = lax.dynamic_slice_in_dim(pair_sum, side * rows, rows, 0)
    other = lax.dynamic_slice_in_dim(pair_sum, (1 - side) * rows, rows, 0).astype(jnp.bfloat16)
    levels = lax.axis_size("rep").bit_length() - 1
    branches = [tail(1 << bit_number, HALVES) for bit_number in range(levels)]
    averaged, momentum_new = lax.switch(
        step_index[0] % levels, branches, own, other, weight[0], momentum[0]
    )
    return (averaged[None], momentum_new[None])


def solution(mesh):
    n_rep, n_shard = mesh.devices.shape
    split = Mesh(
        np.asarray(mesh.devices).reshape(n_rep, n_shard // PAIR, PAIR), ("rep", "z", "xh")
    )
    tokens = ("rep", "z", "xh")
    return jax.shard_map(
        per_device,
        mesh=split,
        in_specs=(
            P(tokens, None),
            P(tokens, None),
            P("rep", ("z", "xh"), None),
            P("rep", ("z", "xh"), None),
            P(),
        ),
        out_specs=(P("rep", ("z", "xh"), None), P("rep", ("z", "xh"), None)),
        check_vma=False,
    )
```

time: 106 us -> 101 us (0.953); the launches traced: 105 us -> 101 us
  waiting for transfers between devices: 68.9 us -> 64.3 us
  other arithmetic: 3.98 us -> 2.09 us
  starting transfers between devices: 12.2 us -> 13.8 us
    ppermute x1 -> x2, starting transfers between devices: 0.61 us -> 3.53 us  [run(): swapped = lax.ppermute(other[lo:lo + step], 'xh', [(0, 1), (1, 0)])]
    ppermute x1 -> x2, waiting for transfers between devices: 11 us -> 8.87 us  [run(): swapped = lax.ppermute(other[lo:lo + step], 'xh', [(0, 1), (1, 0)])]
    ppermute x1 -> x2, waiting for transfers between devices: 9.14 us -> 7.39 us  [from_behind(): lax.ppermute(value, axis, [(i, (i + by) % count) for i in range(count)])]
    convert_element_type x1 -> x3, other arithmetic: 2.06 us -> 0.48 us  [the longest x1 0.34 us: run(): half_step = (weight[lo:lo + step].astype(jnp.float32) - 0.5 * moment.asty...]
    ppermute x1 -> x2, starting transfers between devices: 3.13 us -> 1.81 us  [from_behind(): lax.ppermute(value, axis, [(i, (i + by) % count) for i in range(count)])]
    unnamed x3 -> x7, local copies, waits for them, and re-layouts: 2.28 us -> 2.28 us
  transfers between devices with their start and end apart: 4 -> 6, of which waited for: 4 -> 6; matrix products, arithmetic and copies ran while one was open for 2% -> 3% of each run, Pallas kernels for 0% -> 0%
where the time goes in v4:
time: 101 us
  waiting for transfers between devices  64.3 us (64%)
  between operations  14.7 us (15%)
  starting transfers between devices  13.8 us (14%)
  matrix products  3.14 us (3%)
  local copies, waits for them, and re-layouts  3.06 us (3%)
  other arithmetic  2.09 us (2%)
    all_to_all x1, waiting for transfers between devices, pair_gradient(): columns = lax.all_to_all(columns, 'z', 0, 0)  37.9 us
    all_gather x1, waiting for transfers between devices, pair_gradient(): cot_blocks = lax.all_gather(cotangent, 'z')  9.44 us
    ppermute x2, waiting for transfers between devices, run(): swapped = lax.ppermute(other[lo:lo + step], 'xh', [(0, 1), (1, 0)])  8.87 us
    all_to_all x1, starting transfers between devices, pair_gradient(): columns = lax.all_to_all(columns, 'z', 0, 0)  8.47 us
    ppermute x2, waiting for transfers between devices, from_behind(): lax.ppermute(value, axis, [(i, (i + by) % count) for i in range(count)])  7.39 us
    ppermute x2, starting transfers between devices, run(): swapped = lax.ppermute(other[lo:lo + step], 'xh', [(0, 1), (1, 0)])  3.53 us
    dot_general x1, matrix products, pair_gradient(): jnp.einsum('ktr,ktc->rc', columns, cot_blocks, preferred_element_type=jnp...  3.14 us
    unnamed x7, local copies, waits for them, and re-layouts  2.28 us
  transfers between devices with their start and end apart: 6, of which 6 were waited for; matrix products, arithmetic and copies ran while one was open for 3% of the time, Pallas kernels for 0%

profile of v4, /device:TPU:4, one launch (start us, length us, event | category | flops | bytes accessed | tf_op | source)
XLA Modules:
  0.0 101.2 jit_solution(7110907028521533579)
XLA Ops:
  7.2 0.0 all-gather.3.cloned.1.call-start
  7.2 0.7 all-gather.3.cloned.1.call-update
  7.9 2.3 %copy.23 = bf16[128,4096]{0,1:T(8,128)(2,1)} copy(bf16[128,4096]{1,0:T(8,128)(2,1)} %param.9) | data formatting | bytes 2097152 | tf_op args[0]
  10.2 8.5 %all-to-all-start = ((bf16[8,128,512]{1,2,0:T(8,128)(2,1)}), bf16[8,128,512]{1,2,0:T(8,128)(2,1)S(1)}, u32[]{:S(2)}, u32[]{:S(2)}) async-start(bf16[8,128,512]{1,2,0:T(8,128)(2,1)} %bitcast.26), calls=%async_computation | async-start | bytes 2097152 | tf_op jit(solution)/shard_map/all_to_all | solution.py:21
  19.3 37.9 %all-to-all-done = bf16[8,128,512]{1,2,0:T(8,128)(2,1)S(1)} async-done(((bf16[8,128,512]{1,2,0:T(8,128)(2,1)}), bf16[8,128,512]{1,2,0:T(8,128)(2,1)S(1)}, u32[]{:S(2)}, u32[]{:S(2)}) %all-to-all-start) | async-done | bytes 1048608 | tf_op jit(solution)/shard_map/all_to_all | solution.py:21
  57.2 0.0 copy-start.2
  57.2 9.4 %all-gather.3.cloned.1.call-done = bf16[1024,896]{1,0:T(8,128)(2,1)} async-done(((bf16[128,896]{1,0:T(8,128)(2,1)}), bf16[1024,896]{1,0:T(8,128)(2,1)}) %all-gather.3.cloned.1.call-update) | async-done | bytes 1835024 | tf_op jit(solution)/shard_map/all_gather | solution.py:22
  66.7 0.0 copy-done.2
  66.7 0.0 copy-start
  66.7 0.0 copy-start.1
  66.7 3.1 %convolution_bitcast_fusion = f32[512,896]{1,0:T(8,128)S(1)} fusion(bf16[8,128,512]{1,2,0:T(8,128)(2,1)} %copy-done.2, bf16[8,128,896]{2,1,0:T(8,128)(2,1)} %bitcast.76), kind=kOutput, calls=%fused_computation.56 | convolution fusion | flops 939524096 | bytes 4718592 | tf_op jit(solution)/shard_map/ktr,ktc->rc/dot_general | solution.py:23
  69.8 0.1 dynamic-slice_convert_fusion
  69.9 0.0 copy-done
  69.9 0.0 copy-done.1
  69.9 24.5 %conditional.1 = (bf16[1,256,896]{2,1,0:T(8,128)(2,1)}, bf16[1,256,896]{2,1,0:T(8,128)(2,1)}) conditional(s32[]{:T(128)} %clamp.3, (bf16[1,256,896]{2,1,0:T(8,128)(2,1)S(1)}, bf16[1,256,896]{2,1,0:T(8,128)(2,1)S(1)}, s32[]{:T(128)}, f32[512,896]{1,0:T(8,128)S(1)}, bf16[256,896]{1,0:T(8,128)(2,1)S(1)}, ...), branch_computations={%region_0.1_spmd, %region_1.2_spmd, %region_2.3_spmd, %region_3.4_... | conditional | flops 5505029 | bytes 11010290 | solution.py:62
  69.9 0.7 fusion.32
  70.7 0.5 collective-permute-start
  71.2 3.0 %collective-permute-start.2 = (bf16[128,896]{1,0:T(8,128)(2,1)S(1)}, bf16[128,896]{1,0:T(8,128)(2,1)S(1)}, u32[]{:S(2)}, u32[]{:S(2)}) collective-permute-start(bf16[128,896]{1,0:T(8,128)(2,1)S(1)} %get-tuple-element.153), channel_id=1, source_target_pairs={{0,1},{1,0},{2,3},{3,2},{4,5},{5,4},{6,7},{7,6},{8,9},{9,8},{10,11... | collective-permute-start | bytes 688136 | tf_op jit(solution)/shard_map/cond/branch_0_fun/ppermute | solution.py:34
  74.2 6.4 %collective-permute-done = bf16[128,896]{1,0:T(8,128)(2,1)S(1)} collective-permute-done((bf16[128,896]{1,0:T(8,128)(2,1)}, bf16[128,896]{1,0:T(8,128)(2,1)S(1)}, u32[]{:S(2)}, u32[]{:S(2)}) %collective-permute-start) | collective-permute-done | bytes 229408 | tf_op jit(solution)/shard_map/cond/branch_0_fun/ppermute | solution.py:34
  80.6 2.5 %collective-permute-done.2 = bf16[128,896]{1,0:T(8,128)(2,1)S(1)} collective-permute-done((bf16[128,896]{1,0:T(8,128)(2,1)S(1)}, bf16[128,896]{1,0:T(8,128)(2,1)S(1)}, u32[]{:S(2)}, u32[]{:S(2)}) %collective-permute-start.2) | collective-permute-done | bytes 229408 | tf_op jit(solution)/shard_map/cond/branch_0_fun/ppermute | solution.py:34
  83.1 0.3 fusion.5
  83.4 0.1 collective-permute-start.3
  83.5 1.7 %collective-permute-start.1 = (bf16[128,896]{1,0:T(8,128)(2,1)S(1)}, bf16[128,896]{1,0:T(8,128)(2,1)S(1)}, u32[]{:S(2)}, u32[]{:S(2)}) collective-permute-start(bf16[128,896]{1,0:T(8,128)(2,1)S(1)} %get-tuple-element.134), channel_id=1, source_target_pairs={{0,16},{16,32},{32,48},{48,64},{64,80},{80,96},{96,112},{112,128},... | collective-permute-start | bytes 688136 | tf_op jit(solution)/shard_map/cond/branch_0_fun/ppermute | solution.py:13
  85.2 0.8 maximum_bitcast_fusion.1
  86.0 5.0 %collective-permute-done.3 = bf16[128,896]{1,0:T(8,128)(2,1)S(1)} collective-permute-done((bf16[128,896]{1,0:T(8,128)(2,1)S(1)}, bf16[128,896]{1,0:T(8,128)(2,1)S(1)}, u32[]{:S(2)}, u32[]{:S(2)}) %collective-permute-start.3) | collective-permute-done | bytes 229408 | tf_op jit(solution)/shard_map/cond/branch_0_fun/ppermute | solution.py:13
  91.0 0.1 multiply_convert_fusion
  91.1 2.4 %collective-permute-done.1 = bf16[128,896]{1,0:T(8,128)(2,1)S(1)} collective-permute-done((bf16[128,896]{1,0:T(8,128)(2,1)S(1)}, bf16[128,896]{1,0:T(8,128)(2,1)S(1)}, u32[]{:S(2)}, u32[]{:S(2)}) %collective-permute-start.1) | collective-permute-done | bytes 229408 | tf_op jit(solution)/shard_map/cond/branch_0_fun/ppermute | solution.py:13
  93.5 0.1 multiply_convert_fusion.1
  93.6 0.8 maximum_bitcast_fusion
Async XLA Ops:
  7.2 59.5 %all-gather.3.cloned.1.call-start = ((), (), s32[]{:S(2)}) async-start(), calls=%async_computation.1 | async-start | bytes 2064384 | tf_op jit(solution)/shard_map/all_gather | solution.py:22
  10.2 47.1 %all-to-all-start = ((bf16[8,128,512]{1,2,0:T(8,128)(2,1)}), bf16[8,128,512]{1,2,0:T(8,128)(2,1)S(1)}, u32[]{:S(2)}, u32[]{:S(2)}) async-start(bf16[8,128,512]{1,2,0:T(8,128)(2,1)} %bitcast.26), calls=%async_computation | async-start | bytes 2097152 | tf_op jit(solution)/shard_map/all_to_all | solution.py:21
  57.2 9.4 %copy-start.2 = (bf16[8,128,512]{1,2,0:T(8,128)(2,1)}, bf16[8,128,512]{1,2,0:T(8,128)(2,1)S(1)}, u32[]{:S(2)}) copy-start(bf16[8,128,512]{1,2,0:T(8,128)(2,1)S(1)} %all-to-all-done) | copy-start | bytes 3145732
  66.7 3.2 %copy-start = (bf16[1,256,896]{2,1,0:T(8,128)(2,1)S(1)}, bf16[1,256,896]{2,1,0:T(8,128)(2,1)}, u32[]{:S(2)}) copy-start(bf16[1,256,896]{2,1,0:T(8,128)(2,1)} %param.11) | copy-start | bytes 1376260
  66.7 3.2 %copy-start.1 = (bf16[1,256,896]{2,1,0:T(8,128)(2,1)S(1)}, bf16[1,256,896]{2,1,0:T(8,128)(2,1)}, u32[]{:S(2)}) copy-start(bf16[1,256,896]{2,1,0:T(8,128)(2,1)} %param.12) | copy-start | bytes 1376260
  70.7 9.9 %collective-permute-start = (bf16[128,896]{1,0:T(8,128)(2,1)}, bf16[128,896]{1,0:T(8,128)(2,1)S(1)}, u32[]{:S(2)}, u32[]{:S(2)}) collective-permute-start(bf16[128,896]{1,0:T(8,128)(2,1)} %get-tuple-element.152), channel_id=1, source_target_pairs={{0,1},{1,0},{2,3},{3,2},{4,5},{5,4},{6,7},{7,6},{8,9},{9,8},{10,11... | collective-permute-start | bytes 688136 | tf_op jit(solution)/shard_map/cond/branch_0_fun/ppermute | solution.py:34
  71.2 11.9 %collective-permute-start.2 = (bf16[128,896]{1,0:T(8,128)(2,1)S(1)}, bf16[128,896]{1,0:T(8,128)(2,1)S(1)}, u32[]{:S(2)}, u32[]{:S(2)}) collective-permute-start(bf16[128,896]{1,0:T(8,128)(2,1)S(1)} %get-tuple-element.153), channel_id=1, source_target_pairs={{0,1},{1,0},{2,3},{3,2},{4,5},{5,4},{6,7},{7,6},{8,9},{9,8},{10,11... | collective-permute-start | bytes 688136 | tf_op jit(solution)/shard_map/cond/branch_0_fun/ppermute | solution.py:34
  83.4 7.6 %collective-permute-start.3 = (bf16[128,896]{1,0:T(8,128)(2,1)S(1)}, bf16[128,896]{1,0:T(8,128)(2,1)S(1)}, u32[]{:S(2)}, u32[]{:S(2)}) collective-permute-start(bf16[128,896]{1,0:T(8,128)(2,1)S(1)} %get-tuple-element.150), channel_id=1, source_target_pairs={{0,16},{16,32},{32,48},{48,64},{64,80},{80,96},{96,112},{112,128},... | collective-permute-start | bytes 688136 | tf_op jit(solution)/shard_map/cond/branch_0_fun/ppermute | solution.py:13
  83.5 10.0 %collective-permute-start.1 = (bf16[128,896]{1,0:T(8,128)(2,1)S(1)}, bf16[128,896]{1,0:T(8,128)(2,1)S(1)}, u32[]{:S(2)}, u32[]{:S(2)}) collective-permute-start(bf16[128,896]{1,0:T(8,128)(2,1)S(1)} %get-tuple-element.134), channel_id=1, source_target_pairs={{0,16},{16,32},{32,48},{48,64},{64,80},{80,96},{96,112},{112,128},... | collective-permute-start | bytes 688136 | tf_op jit(solution)/shard_map/cond/branch_0_fun/ppermute | solution.py:13
Sparse Core Ops, SparseCore 0:
  9.8 56.8 all-gather.2

commit v5 on v4

--- a/solution.py
+++ b/solution.py
@@ -26,12 +26,12 @@
 
 
 def tail(distance, halves):
-    def run(own, other, weight, momentum):
+    def run(own, others, weight, momentum):
         rows = own.shape[0]
         step = rows // halves
         averaged, momentum_new = [], []
-        for lo in range(0, rows, step):
-            swapped = lax.ppermute(other[lo : lo + step], "xh", [(0, 1), (1, 0)])
+        for piece, lo in zip(others, range(0, rows, step)):
+            swapped = lax.ppermute(piece, "xh", [(0, 1), (1, 0)])
             gradient = own[lo : lo + step] + swapped.astype(jnp.float32)
             moment = (0.9 * momentum[lo : lo + step].astype(jnp.float32) + gradient).astype(
                 jnp.bfloat16
@@ -56,11 +56,15 @@
     pair_sum = pair_gradient(activations, cotangent, rows)
     side = lax.axis_index("xh")
     own = lax.dynamic_slice_in_dim(pair_sum, side * rows, rows, 0)
-    other = lax.dynamic_slice_in_dim(pair_sum, (1 - side) * rows, rows, 0).astype(jnp.bfloat16)
+    step = rows // HALVES
+    others = tuple(
+        lax.dynamic_slice_in_dim(pair_sum, (1 - side) * rows + lo, step, 0).astype(jnp.bfloat16)
+        for lo in range(0, rows, step)
+    )
     levels = lax.axis_size("rep").bit_length() - 1
     branches = [tail(1 << bit_number, HALVES) for bit_number in range(levels)]
     averaged, momentum_new = lax.switch(
-        step_index[0] % levels, branches, own, other, weight[0], momentum[0]
+        step_index[0] % levels, branches, own, others, weight[0], momentum[0]
     )
     return (averaged[None], momentum_new[None])
 

time: 101 us -> 102 us (level)
  starting transfers between devices: 13.8 us -> 15.2 us
    ppermute x2, starting transfers between devices: 1.81 us -> 3.15 us  [from_behind(): lax.ppermute(value, axis, [(i, (i + by) % count) for i in range(count)])]
where the time goes in v5:
time: 102 us; the launch traced here: 103 us
  waiting for transfers between devices  64.8 us (64%)
  starting transfers between devices  15.2 us (15%)
  between operations  14.7 us (14%)
  matrix products  3.14 us (3%)
  local copies, waits for them, and re-layouts  3.04 us (3%)
  other arithmetic  2.09 us (2%)
    all_to_all x1, waiting for transfers between devices, pair_gradient(): columns = lax.all_to_all(columns, 'z', 0, 0)  37.9 us
    all_gather x1, waiting for transfers between devices, pair_gradient(): cot_blocks = lax.all_gather(cotangent, 'z')  9.44 us
    ppermute x2, waiting for transfers between devices, run(): swapped = lax.ppermute(piece, 'xh', [(0, 1), (1, 0)])  8.87 us
    all_to_all x1, starting transfers between devices, pair_gradient(): columns = lax.all_to_all(columns, 'z', 0, 0)  8.47 us
    ppermute x2, waiting for transfers between devices, from_behind(): lax.ppermute(value, axis, [(i, (i + by) % count) for i in range(count)])  7.92 us
    ppermute x2, starting transfers between devices, run(): swapped = lax.ppermute(piece, 'xh', [(0, 1), (1, 0)])  3.53 us
    ppermute x2, starting transfers between devices, from_behind(): lax.ppermute(value, axis, [(i, (i + by) % count) for i in range(count)])  3.15 us
    dot_general x1, matrix products, pair_gradient(): jnp.einsum('ktr,ktc->rc', columns, cot_blocks, preferred_element_type=jnp...  3.14 us
  transfers between devices with their start and end apart: 6, of which 6 were waited for; matrix products, arithmetic and copies ran while one was open for 3% of the time, Pallas kernels for 0%

profile of v5, /device:TPU:4, one launch (start us, length us, event | category | flops | bytes accessed | tf_op | source)
XLA Modules:
  0.0 103.0 jit_solution(9940959693422995624)
XLA Ops:
  7.2 0.0 all-gather.3.cloned.1.call-start
  7.2 0.7 all-gather.3.cloned.1.call-update
  7.9 2.3 %copy.23 = bf16[128,4096]{0,1:T(8,128)(2,1)} copy(bf16[128,4096]{1,0:T(8,128)(2,1)} %param.9) | data formatting | bytes 2097152 | tf_op args[0]
  10.2 8.5 %all-to-all-start = ((bf16[8,128,512]{1,2,0:T(8,128)(2,1)}), bf16[8,128,512]{1,2,0:T(8,128)(2,1)S(1)}, u32[]{:S(2)}, u32[]{:S(2)}) async-start(bf16[8,128,512]{1,2,0:T(8,128)(2,1)} %bitcast.26), calls=%async_computation | async-start | bytes 2097152 | tf_op jit(solution)/shard_map/all_to_all | solution.py:21
  19.3 37.9 %all-to-all-done = bf16[8,128,512]{1,2,0:T(8,128)(2,1)S(1)} async-done(((bf16[8,128,512]{1,2,0:T(8,128)(2,1)}), bf16[8,128,512]{1,2,0:T(8,128)(2,1)S(1)}, u32[]{:S(2)}, u32[]{:S(2)}) %all-to-all-start) | async-done | bytes 1048608 | tf_op jit(solution)/shard_map/all_to_all | solution.py:21
  57.2 0.0 copy-start.2
  57.2 9.4 %all-gather.3.cloned.1.call-done = bf16[1024,896]{1,0:T(8,128)(2,1)} async-done(((bf16[128,896]{1,0:T(8,128)(2,1)}), bf16[1024,896]{1,0:T(8,128)(2,1)}) %all-gather.3.cloned.1.call-update) | async-done | bytes 1835024 | tf_op jit(solution)/shard_map/all_gather | solution.py:22
  66.7 0.0 copy-done.2
  66.7 0.0 copy-start
  66.7 0.0 copy-start.1
  66.7 3.1 %convolution_bitcast_fusion = f32[512,896]{1,0:T(8,128)S(1)} fusion(bf16[8,128,512]{1,2,0:T(8,128)(2,1)} %copy-done.2, bf16[8,128,896]{2,1,0:T(8,128)(2,1)} %bitcast.76), kind=kOutput, calls=%fused_computation.56 | convolution fusion | flops 939524096 | bytes 4718592 | tf_op jit(solution)/shard_map/ktr,ktc->rc/dot_general | solution.py:23
  69.8 0.7 dynamic-slice_convert_fusion
  70.6 0.0 copy-done
  70.6 0.0 copy-done.1
  70.6 25.6 %conditional.1 = (bf16[1,256,896]{2,1,0:T(8,128)(2,1)}, bf16[1,256,896]{2,1,0:T(8,128)(2,1)}) conditional(s32[]{:T(128)} %clamp.3, (bf16[1,256,896]{2,1,0:T(8,128)(2,1)S(1)}, bf16[1,256,896]{2,1,0:T(8,128)(2,1)S(1)}, s32[]{:T(128)}, f32[512,896]{1,0:T(8,128)S(1)}, bf16[128,896]{1,0:T(8,128)(2,1)}, ...), branch_computations={%region_0.1_spmd, %region_1.2_spmd, %region_2.3_spmd, %region_3.4_... | conditional | flops 5505029 | bytes 10092786 | solution.py:66
  70.6 0.5 collective-permute-start.4
  71.1 3.0 %collective-permute-start.6 = (bf16[128,896]{1,0:T(8,128)(2,1)S(1)}, bf16[128,896]{1,0:T(8,128)(2,1)S(1)}, u32[]{:S(2)}, u32[]{:S(2)}) collective-permute-start(bf16[128,896]{1,0:T(8,128)(2,1)S(1)} %get-tuple-element.105), channel_id=1, source_target_pairs={{0,1},{1,0},{2,3},{3,2},{4,5},{5,4},{6,7},{7,6},{8,9},{9,8},{10,11... | collective-permute-start | bytes 688136 | tf_op jit(solution)/shard_map/cond/branch_1_fun/ppermute | solution.py:34
  74.1 6.4 %collective-permute-done.4 = bf16[128,896]{1,0:T(8,128)(2,1)S(1)} collective-permute-done((bf16[128,896]{1,0:T(8,128)(2,1)}, bf16[128,896]{1,0:T(8,128)(2,1)S(1)}, u32[]{:S(2)}, u32[]{:S(2)}) %collective-permute-start.4) | collective-permute-done | bytes 229408 | tf_op jit(solution)/shard_map/cond/branch_1_fun/ppermute | solution.py:34
  80.5 2.5 %collective-permute-done.6 = bf16[128,896]{1,0:T(8,128)(2,1)S(1)} collective-permute-done((bf16[128,896]{1,0:T(8,128)(2,1)S(1)}, bf16[128,896]{1,0:T(8,128)(2,1)S(1)}, u32[]{:S(2)}, u32[]{:S(2)}) %collective-permute-start.6) | collective-permute-done | bytes 229408 | tf_op jit(solution)/shard_map/cond/branch_1_fun/ppermute | solution.py:34
  83.0 0.3 fusion.11
  83.3 1.7 %collective-permute-start.7 = (bf16[128,896]{1,0:T(8,128)(2,1)S(1)}, bf16[128,896]{1,0:T(8,128)(2,1)S(1)}, u32[]{:S(2)}, u32[]{:S(2)}) collective-permute-start(bf16[128,896]{1,0:T(8,128)(2,1)S(1)} %get-tuple-element.164), channel_id=1, source_target_pairs={{0,32},{16,48},{32,64},{48,80},{64,96},{80,112},{96,128},{112,144}... | collective-permute-start | bytes 688136 | tf_op jit(solution)/shard_map/cond/branch_1_fun/ppermute | solution.py:13
  85.0 1.5 %collective-permute-start.5 = (bf16[128,896]{1,0:T(8,128)(2,1)S(1)}, bf16[128,896]{1,0:T(8,128)(2,1)S(1)}, u32[]{:S(2)}, u32[]{:S(2)}) collective-permute-start(bf16[128,896]{1,0:T(8,128)(2,1)S(1)} %get-tuple-element.150), channel_id=1, source_target_pairs={{0,32},{16,48},{32,64},{48,80},{64,96},{80,112},{96,128},{112,144}... | collective-permute-start | bytes 688136 | tf_op jit(solution)/shard_map/cond/branch_1_fun/ppermute | solution.py:13
  86.5 0.8 maximum_bitcast_fusion.3
  87.3 5.5 %collective-permute-done.7 = bf16[128,896]{1,0:T(8,128)(2,1)S(1)} collective-permute-done((bf16[128,896]{1,0:T(8,128)(2,1)S(1)}, bf16[128,896]{1,0:T(8,128)(2,1)S(1)}, u32[]{:S(2)}, u32[]{:S(2)}) %collective-permute-start.7) | collective-permute-done | bytes 229408 | tf_op jit(solution)/shard_map/cond/branch_1_fun/ppermute | solution.py:13
  92.8 0.1 multiply_convert_fusion.2
  92.9 2.4 %collective-permute-done.5 = bf16[128,896]{1,0:T(8,128)(2,1)S(1)} collective-permute-done((bf16[128,896]{1,0:T(8,128)(2,1)S(1)}, bf16[128,896]{1,0:T(8,128)(2,1)S(1)}, u32[]{:S(2)}, u32[]{:S(2)}) %collective-permute-start.5) | collective-permute-done | bytes 229408 | tf_op jit(solution)/shard_map/cond/branch_1_fun/ppermute | solution.py:13
  95.3 0.1 multiply_convert_fusion.3
  95.4 0.8 maximum_bitcast_fusion.2
Async XLA Ops:
  7.2 59.5 %all-gather.3.cloned.1.call-start = ((), (), s32[]{:S(2)}) async-start(), calls=%async_computation.1 | async-start | bytes 2064384 | tf_op jit(solution)/shard_map/all_gather | solution.py:22
  10.2 47.1 %all-to-all-start = ((bf16[8,128,512]{1,2,0:T(8,128)(2,1)}), bf16[8,128,512]{1,2,0:T(8,128)(2,1)S(1)}, u32[]{:S(2)}, u32[]{:S(2)}) async-start(bf16[8,128,512]{1,2,0:T(8,128)(2,1)} %bitcast.26), calls=%async_computation | async-start | bytes 2097152 | tf_op jit(solution)/shard_map/all_to_all | solution.py:21
  57.2 9.4 %copy-start.2 = (bf16[8,128,512]{1,2,0:T(8,128)(2,1)}, bf16[8,128,512]{1,2,0:T(8,128)(2,1)S(1)}, u32[]{:S(2)}) copy-start(bf16[8,128,512]{1,2,0:T(8,128)(2,1)S(1)} %all-to-all-done) | copy-start | bytes 3145732
  66.7 3.9 %copy-start = (bf16[1,256,896]{2,1,0:T(8,128)(2,1)S(1)}, bf16[1,256,896]{2,1,0:T(8,128)(2,1)}, u32[]{:S(2)}) copy-start(bf16[1,256,896]{2,1,0:T(8,128)(2,1)} %param.11) | copy-start | bytes 1376260
  66.7 3.9 %copy-start.1 = (bf16[1,256,896]{2,1,0:T(8,128)(2,1)S(1)}, bf16[1,256,896]{2,1,0:T(8,128)(2,1)}, u32[]{:S(2)}) copy-start(bf16[1,256,896]{2,1,0:T(8,128)(2,1)} %param.12) | copy-start | bytes 1376260
  70.6 9.9 %collective-permute-start.4 = (bf16[128,896]{1,0:T(8,128)(2,1)}, bf16[128,896]{1,0:T(8,128)(2,1)S(1)}, u32[]{:S(2)}, u32[]{:S(2)}) collective-permute-start(bf16[128,896]{1,0:T(8,128)(2,1)} %get-tuple-element.104), channel_id=1, source_target_pairs={{0,1},{1,0},{2,3},{3,2},{4,5},{5,4},{6,7},{7,6},{8,9},{9,8},{10,11... | collective-permute-start | bytes 688136 | tf_op jit(solution)/shard_map/cond/branch_1_fun/ppermute | solution.py:34
  71.1 11.9 %collective-permute-start.6 = (bf16[128,896]{1,0:T(8,128)(2,1)S(1)}, bf16[128,896]{1,0:T(8,128)(2,1)S(1)}, u32[]{:S(2)}, u32[]{:S(2)}) collective-permute-start(bf16[128,896]{1,0:T(8,128)(2,1)S(1)} %get-tuple-element.105), channel_id=1, source_target_pairs={{0,1},{1,0},{2,3},{3,2},{4,5},{5,4},{6,7},{7,6},{8,9},{9,8},{10,11... | collective-permute-start | bytes 688136 | tf_op jit(solution)/shard_map/cond/branch_1_fun/ppermute | solution.py:34
  83.3 9.5 %collective-permute-start.7 = (bf16[128,896]{1,0:T(8,128)(2,1)S(1)}, bf16[128,896]{1,0:T(8,128)(2,1)S(1)}, u32[]{:S(2)}, u32[]{:S(2)}) collective-permute-start(bf16[128,896]{1,0:T(8,128)(2,1)S(1)} %get-tuple-element.164), channel_id=1, source_target_pairs={{0,32},{16,48},{32,64},{48,80},{64,96},{80,112},{96,128},{112,144}... | collective-permute-start | bytes 688136 | tf_op jit(solution)/shard_map/cond/branch_1_fun/ppermute | solution.py:13
  85.0 10.3 %collective-permute-start.5 = (bf16[128,896]{1,0:T(8,128)(2,1)S(1)}, bf16[128,896]{1,0:T(8,128)(2,1)S(1)}, u32[]{:S(2)}, u32[]{:S(2)}) collective-permute-start(bf16[128,896]{1,0:T(8,128)(2,1)S(1)} %get-tuple-element.150), channel_id=1, source_target_pairs={{0,32},{16,48},{32,64},{48,80},{64,96},{80,112},{96,128},{112,144}... | collective-permute-start | bytes 688136 | tf_op jit(solution)/shard_map/cond/branch_1_fun/ppermute | solution.py:13
Sparse Core Ops, SparseCore 0:
  9.8 56.8 all-gather.2
